TPU v7x, 32 devices: a whole 2x2x4 slice. The times are simulated.
32 devices in a mesh: parts: 2 (over x), chain: 16 (over z, y, core).
Axes of the slice: x: 2, y: 2, z: 4, core: 2. Of those that a mesh axis runs over, the one named last changes fastest.
Arguments:
- subspace: float32 [64, 8192], P('parts', 'chain'), parts along dimension 0, may hold values from -4 to 4
- s_inv: float32 [8, 32, 2, 256, 256], P('parts', 'chain'), parts along dimension 0, may hold values from -1 to 1
- couple: float32 [32, 512, 256], P('chain', 'parts'), parts along dimension 1, may hold values from -1 to 1
- diag_blocks: float32 [32, 512, 256], P('chain', 'parts'), parts along dimension 1, may hold values from -4 to 4
- weights: float32 [8, 2], P('parts'), parts along dimension 0, may hold values from -1 to 1
Outputs:
- filtered: float32 [64, 8192], P('parts', 'chain'), parts along dimension 0
- applied: float32 [64, 8192], P('parts', 'chain'), parts along dimension 0
- grams: float32 [2, 64, 32], P(None, 'parts'), parts along dimension 1
There are 2 independent parts, one for each index of `parts`. A program takes and returns all parts, laid end to end along the dimension named above; each array names one. Nothing has to cross between parts.
All inputs are finite; a program needn't handle non-finite values.
Results may differ from a plain program's by a relative error of at most 0.00027.
Values sent between devices are 32-bit elements; how exact they have to be, the bound alone decides.
No kernel may reach another device: no remote copies, remote signals or barrier semaphores. Data moves between devices by JAX's collectives and lax.ppermute only.
A program may use at most 192 MiB of HBM per device.

v0:
```python
import jax
import jax.numpy as jnp
from jax import lax
from jax.sharding import PartitionSpec as P

highest = lax.Precision.HIGHEST


def passed_along(shard, axis, by):
    peers = lax.axis_size(axis)
    pairs = [(i, i + by) for i in range(peers) if 0 <= i + by < peers]
    return lax.ppermute(shard, axis, pairs)


def inverse_apply(pivot_inv, vecs):
    real_part = jnp.einsum(
        "qnk,qjk->qnj", vecs[:, 0], pivot_inv[:, 0], precision=highest
    ) - jnp.einsum("qnk,qjk->qnj", vecs[:, 1], pivot_inv[:, 1], precision=highest)
    imag_part = jnp.einsum(
        "qnk,qjk->qnj", vecs[:, 0], pivot_inv[:, 1], precision=highest
    ) + jnp.einsum("qnk,qjk->qnj", vecs[:, 1], pivot_inv[:, 0], precision=highest)
    return jnp.stack([real_part, imag_part], axis=1)


def right_apply(vecs, matrix):
    real_part = jnp.einsum(
        "qnk,qkj->qnj", vecs[:, 0], matrix[:, 0], precision=highest
    ) - jnp.einsum("qnk,qkj->qnj", vecs[:, 1], matrix[:, 1], precision=highest)
    imag_part = jnp.einsum(
        "qnk,qkj->qnj", vecs[:, 0], matrix[:, 1], precision=highest
    ) + jnp.einsum("qnk,qkj->qnj", vecs[:, 1], matrix[:, 0], precision=highest)
    return jnp.stack([real_part, imag_part], axis=1)


def couple_down(coupling_blk, vecs):
    return jnp.einsum("qcnk,kj->qcnj", vecs, coupling_blk, precision=highest)


def couple_up(coupling_blk, vecs):
    return jnp.einsum("qcnk,jk->qcnj", vecs, coupling_blk, precision=highest)


def sweep_forward(pivots, couple, start_rows, source, store_all):
    blocks_dev = couple.shape[0]

    def advance(carried, position):
        pivot_inv = lax.dynamic_index_in_dim(pivots, position, 1, keepdims=False)
        coupling_blk = lax.dynamic_index_in_dim(couple, position, 0, keepdims=False)
        combined = carried
        if source is not None:
            rhs_block = lax.dynamic_index_in_dim(source, position, 0, keepdims=False)
            combined = combined.at[:, 0].add(rhs_block[None])
        solved = inverse_apply(pivot_inv, combined)
        return (couple_down(coupling_blk, solved), solved if store_all else None)

    return lax.scan(advance, start_rows, jnp.arange(blocks_dev))


def sweep_backward(pivots, couple, start_rows, solved_all, store_all):
    blocks_dev = couple.shape[0]

    def retreat(carried, position):
        pivot_inv = lax.dynamic_index_in_dim(pivots, position, 1, keepdims=False)
        coupling_blk = lax.dynamic_index_in_dim(couple, position, 0, keepdims=False)
        correction = inverse_apply(pivot_inv, couple_up(coupling_blk, carried))
        if solved_all is not None:
            correction = (
                lax.dynamic_index_in_dim(solved_all, position, 0, keepdims=False) + correction
            )
        return (correction, correction if store_all else None)

    return lax.scan(retreat, start_rows, jnp.arange(blocks_dev), reverse=True)


def shards(subspace, s_inv, couple, diag_blocks, weights):
    points = s_inv.shape[0]
    blocks_dev = couple.shape[0]
    block_width = couple.shape[1]
    vectors = subspace.shape[0]
    source = subspace.reshape(vectors, blocks_dev, block_width).transpose(1, 0, 2)
    zero_rows = jnp.zeros((points, 2, vectors, block_width), jnp.float32)
    plain_eye = jnp.stack(
        [
            jnp.eye(block_width, dtype=jnp.float32),
            jnp.zeros((block_width, block_width), jnp.float32),
        ]
    )
    identity_map = jnp.broadcast_to(plain_eye, (points, 2, block_width, block_width))
    chain_size = lax.axis_size("chain")
    forward_map, _ = sweep_forward(s_inv, couple, identity_map, None, False)
    forward_tip, _ = sweep_forward(s_inv, couple, zero_rows, source, False)

    def forward_hop(hop_index, inbound):
        return passed_along(right_apply(inbound, forward_map) + forward_tip, "chain", 1)

    incoming = lax.fori_loop(0, chain_size - 1, forward_hop, zero_rows)
    _, solved_all = sweep_forward(s_inv, couple, incoming, source, True)
    backward_map, _ = sweep_backward(s_inv, couple, identity_map, None, False)
    backward_tip, _ = sweep_backward(s_inv, couple, zero_rows, solved_all, False)

    def backward_hop(hop_index, inbound):
        return passed_along(right_apply(inbound, backward_map) + backward_tip, "chain", -1)

    outgoing = lax.fori_loop(0, chain_size - 1, backward_hop, zero_rows)
    _, result = sweep_backward(s_inv, couple, outgoing, solved_all, True)
    signed = weights * jnp.array([1.0, -1.0], jnp.float32)
    filtered_blocks = jnp.einsum("rqcnk,qc->rnk", result, signed, precision=highest)
    down_all = jnp.einsum("rnk,rkj->rnj", filtered_blocks, couple, precision=highest)
    from_next = passed_along(filtered_blocks[0], "chain", -1)
    from_prior = passed_along(down_all[-1], "chain", 1)
    diag_term = jnp.einsum("rnk,rjk->rnj", filtered_blocks, diag_blocks, precision=highest)
    upper_rows = jnp.concatenate([filtered_blocks[1:], from_next[None]], axis=0)
    term_up = jnp.einsum("rnk,rjk->rnj", upper_rows, couple, precision=highest)
    lower_rows = jnp.concatenate([from_prior[None], down_all[:-1]], axis=0)
    applied_blocks = diag_term + term_up + lower_rows
    gram_plain = jnp.einsum("rnk,rmk->nm", filtered_blocks, filtered_blocks, precision=highest)
    gram_matrix = jnp.einsum("rnk,rmk->nm", filtered_blocks, applied_blocks, precision=highest)
    summed = lax.psum(jnp.stack([gram_plain, gram_matrix]), "chain")
    grams = summed / (blocks_dev * block_width * chain_size)
    filtered = filtered_blocks.transpose(1, 0, 2).reshape(vectors, blocks_dev * block_width)
    applied = applied_blocks.transpose(1, 0, 2).reshape(vectors, blocks_dev * block_width)
    return (filtered, applied, grams)


def solution(mesh):
    placed = (
        P("parts", "chain"),
        P("parts", "chain", None, None, None),
        P("chain", "parts", None),
        P("chain", "parts", None),
        P("parts", None),
    )
    return jax.shard_map(
        shards,
        mesh=mesh,
        in_specs=placed,
        out_specs=(P("parts", "chain"), P("parts", "chain"), P(None, "parts", None)),
        check_vma=False,
    )
```

profile of v0, /device:TPU:0, one launch (start us, length us, event | category | flops | bytes accessed | tf_op | source)
XLA Modules:
  0.0 591.9 jit_solution(1425416484922783797)
XLA Ops:
  6.5 25.1 %while.104 = (s32[]{:T(128)}, f32[4,2,256,256]{3,2,1,0:T(8,128)S(1)}, s32[2]{0:T(128)S(1)}, f32[4,2,2,256,256]{4,3,0,2,1:T(8,128)}, f32[2,256,256]{2,1,0:T(8,128)S(1)}, /*index=5*/s32[]{:T(128)}, s32[]{:T(128)}, s32[]{:T(128)}) while((s32[]{:T(128)}, f32[4,2,256,256]{3,2,1,0:T(8,128)S(1)}, s32[2]{0:T(128)S(1)}, ...), condition=%wide.region_3.4_spmd, body=%wide.region_2.3_spmd.sunk | while | flops 4832886784 | bytes 23330956 | solution.py:56
  33.3 18.8 %while.105 = (s32[]{:T(128)}, f32[4,2,32,256]{3,2,1,0:T(8,128)S(1)}, s32[2]{0:T(128)S(1)}, f32[2,32,256]{2,1,0:T(8,128)S(1)}, f32[4,2,2,256,256]{4,3,0,2,1:T(8,1...) while((s32[]{:T(128)}, f32[4,2,32,256]{3,2,1,0:T(8,128)S(1)}, s32[2]{0:T(128)S(1)}, ...), condition=%wide.region_5.6_spmd, body=%wide.region_4.5_spmd.sunk | while | flops 604176384 | bytes 10616983 | solution.py:56
  52.9 173.2 %while.106 = (s32[]{:T(128)}, f32[4,2,32,256]{3,2,0,1:T(8,128)S(1)}, f32[4,2,256,256]{3,2,0,1:T(8,128)S(1)}, f32[4,2,32,256]{3,2,0,1:T(8,128)}, s32[]{:T(128)}) while((s32[]{:T(128)}, f32[4,2,32,256]{3,2,0,1:T(8,128)S(1)}, f32[4,2,256,256]{3,2,0,1:T(8,128)S(1)}, f32[4,2,32,256]{3,2,0,1:T(8,128)}, s32[]{:T(128)}) %tuple.236), condition=%wide.region_7.8_spmd, body=%wide.region_6.7_spmd.sunk | while | flops 402849792 | bytes 8388737 | solution.py:96
  167.7 7.4 %collective-permute-start = (f32[4,2,32,256]{3,2,0,1:T(8,128)}, f32[4,2,32,256]{3,2,0,1:T(8,128)S(1)}, u32[]{:S(2)}, u32[]{:S(2)}) collective-permute-start(f32[4,2,32,256]{3,2,0,1:T(8,128)} %maximum_add_fusion.10), channel_id=1, source_target_pairs={{0,1},{1,2},{2,3},{3,4},{4,5},{5,6},{6,7},{7,8},{8,9},{9,10},{10,1... | collective-permute-start | bytes 786440 | tf_op jit(solution)/shard_map/while/body/eval_jaxpr/ppermute | solution.py:12
  226.1 18.2 %while.107 = (s32[]{:T(128)}, f32[4,2,32,256]{3,2,1,0:T(8,128)S(1)}, f32[2,4,2,32,256]{4,3,1,2,0:T(8,128)}, s32[2]{0:T(128)S(1)}, f32[2,32,256]{2,1,0:T(8,128)S(...) while((s32[]{:T(128)}, f32[4,2,32,256]{3,2,1,0:T(8,128)S(1)}, ...), condition=%wide.region_9.10_spmd, body=%wide.region_8.9_spmd.sunk | while | flops 604241920 | bytes 15335643 | solution.py:56
  244.3 19.8 %while.110 = (s32[]{:T(128)}, f32[4,2,32,256]{3,2,0,1:T(8,128)}, s32[2]{0:T(128)S(1)}, f32[2,4,2,32,256]{4,3,1,2,0:T(8,128)}, f32[2,256,256]{2,1,0:T(8,128)S(1)}...) while((s32[]{:T(128)}, f32[4,2,32,256]{3,2,0,1:T(8,128)}, ...), condition=%wide.region_11.12_spmd.clone, body=%wide.region_10.11_spmd.clone.sunk | while | flops 604241920 | bytes 13369545 | solution.py:72
  265.3 27.5 %while.103 = (s32[]{:T(128)}, f32[4,2,256,256]{3,2,0,1:T(8,128)S(1)}, s32[2]{0:T(128)S(1)}, f32[2,256,256]{2,1,0:T(8,128)S(1)}, f32[4,2,2,256,256]{4,3,0,2,1:T(8,128)}, /*index=5*/s32[]{:T(128)}, s32[]{:T(128)}, s32[]{:T(128)}) while((s32[]{:T(128)}, f32[4,2,256,256]{3,2,0,1:T(8,128)S(1)}, s32[2]{0:T(128)S(1)}, f32[2,256,256]{2,1,0:T(8,128)S(1)}, ...), condition=%wide.region_1.2_spmd, body=%wide.region_0.1_spmd.sunk | while | flops 4832886784 | bytes 27525272 | solution.py:72
  292.9 201.3 %while.108 = (s32[]{:T(128)}, f32[4,2,32,256]{3,2,0,1:T(8,128)S(1)}, f32[4,2,256,256]{3,2,0,1:T(8,128)S(1)}, f32[4,2,32,256]{3,2,0,1:T(8,128)}, s32[]{:T(128)}) while((s32[]{:T(128)}, f32[4,2,32,256]{3,2,0,1:T(8,128)S(1)}, f32[4,2,256,256]{3,2,0,1:T(8,128)S(1)}, f32[4,2,32,256]{3,2,0,1:T(8,128)}, s32[]{:T(128)}) %tuple.225), condition=%wide.region_13.14_spmd, body=%wide.region_12.13_spmd.sunk | while | flops 402849792 | bytes 7340133 | solution.py:104
  312.2 8.1 %collective-permute-done.1 = f32[4,2,32,256]{3,2,0,1:T(8,128)S(1)} collective-permute-done((f32[4,2,32,256]{3,2,0,1:T(8,128)}, f32[4,2,32,256]{3,2,0,1:T(8,128)S(1)}, u32[]{:S(2)}, u32[]{:S(2)}) %collective-permute-start.1) | collective-permute-done | bytes 262176 | tf_op jit(solution)/shard_map/while/body/eval_jaxpr/ppermute | solution.py:12
  339.3 8.1 %collective-permute-done.1 = f32[4,2,32,256]{3,2,0,1:T(8,128)S(1)} collective-permute-done((f32[4,2,32,256]{3,2,0,1:T(8,128)}, f32[4,2,32,256]{3,2,0,1:T(8,128)S(1)}, u32[]{:S(2)}, u32[]{:S(2)}) %collective-permute-start.1) | collective-permute-done | bytes 262176 | tf_op jit(solution)/shard_map/while/body/eval_jaxpr/ppermute | solution.py:12
  353.3 7.5 %collective-permute-done.1 = f32[4,2,32,256]{3,2,0,1:T(8,128)S(1)} collective-permute-done((f32[4,2,32,256]{3,2,0,1:T(8,128)}, f32[4,2,32,256]{3,2,0,1:T(8,128)S(1)}, u32[]{:S(2)}, u32[]{:S(2)}) %collective-permute-start.1) | collective-permute-done | bytes 262176 | tf_op jit(solution)/shard_map/while/body/eval_jaxpr/ppermute | solution.py:12
  366.6 7.5 %collective-permute-done.1 = f32[4,2,32,256]{3,2,0,1:T(8,128)S(1)} collective-permute-done((f32[4,2,32,256]{3,2,0,1:T(8,128)}, f32[4,2,32,256]{3,2,0,1:T(8,128)S(1)}, u32[]{:S(2)}, u32[]{:S(2)}) %collective-permute-start.1) | collective-permute-done | bytes 262176 | tf_op jit(solution)/shard_map/while/body/eval_jaxpr/ppermute | solution.py:12
  380.0 7.5 %collective-permute-done.1 = f32[4,2,32,256]{3,2,0,1:T(8,128)S(1)} collective-permute-done((f32[4,2,32,256]{3,2,0,1:T(8,128)}, f32[4,2,32,256]{3,2,0,1:T(8,128)S(1)}, u32[]{:S(2)}, u32[]{:S(2)}) %collective-permute-start.1) | collective-permute-done | bytes 262176 | tf_op jit(solution)/shard_map/while/body/eval_jaxpr/ppermute | solution.py:12
  393.3 7.5 %collective-permute-done.1 = f32[4,2,32,256]{3,2,0,1:T(8,128)S(1)} collective-permute-done((f32[4,2,32,256]{3,2,0,1:T(8,128)}, f32[4,2,32,256]{3,2,0,1:T(8,128)S(1)}, u32[]{:S(2)}, u32[]{:S(2)}) %collective-permute-start.1) | collective-permute-done | bytes 262176 | tf_op jit(solution)/shard_map/while/body/eval_jaxpr/ppermute | solution.py:12
  406.7 7.5 %collective-permute-done.1 = f32[4,2,32,256]{3,2,0,1:T(8,128)S(1)} collective-permute-done((f32[4,2,32,256]{3,2,0,1:T(8,128)}, f32[4,2,32,256]{3,2,0,1:T(8,128)S(1)}, u32[]{:S(2)}, u32[]{:S(2)}) %collective-permute-start.1) | collective-permute-done | bytes 262176 | tf_op jit(solution)/shard_map/while/body/eval_jaxpr/ppermute | solution.py:12
  420.0 7.5 %collective-permute-done.1 = f32[4,2,32,256]{3,2,0,1:T(8,128)S(1)} collective-permute-done((f32[4,2,32,256]{3,2,0,1:T(8,128)}, f32[4,2,32,256]{3,2,0,1:T(8,128)S(1)}, u32[]{:S(2)}, u32[]{:S(2)}) %collective-permute-start.1) | collective-permute-done | bytes 262176 | tf_op jit(solution)/shard_map/while/body/eval_jaxpr/ppermute | solution.py:12
  433.3 7.5 %collective-permute-done.1 = f32[4,2,32,256]{3,2,0,1:T(8,128)S(1)} collective-permute-done((f32[4,2,32,256]{3,2,0,1:T(8,128)}, f32[4,2,32,256]{3,2,0,1:T(8,128)S(1)}, u32[]{:S(2)}, u32[]{:S(2)}) %collective-permute-start.1) | collective-permute-done | bytes 262176 | tf_op jit(solution)/shard_map/while/body/eval_jaxpr/ppermute | solution.py:12
  446.7 7.5 %collective-permute-done.1 = f32[4,2,32,256]{3,2,0,1:T(8,128)S(1)} collective-permute-done((f32[4,2,32,256]{3,2,0,1:T(8,128)}, f32[4,2,32,256]{3,2,0,1:T(8,128)S(1)}, u32[]{:S(2)}, u32[]{:S(2)}) %collective-permute-start.1) | collective-permute-done | bytes 262176 | tf_op jit(solution)/shard_map/while/body/eval_jaxpr/ppermute | solution.py:12
  460.0 7.5 %collective-permute-done.1 = f32[4,2,32,256]{3,2,0,1:T(8,128)S(1)} collective-permute-done((f32[4,2,32,256]{3,2,0,1:T(8,128)}, f32[4,2,32,256]{3,2,0,1:T(8,128)S(1)}, u32[]{:S(2)}, u32[]{:S(2)}) %collective-permute-start.1) | collective-permute-done | bytes 262176 | tf_op jit(solution)/shard_map/while/body/eval_jaxpr/ppermute | solution.py:12
  473.3 7.5 %collective-permute-done.1 = f32[4,2,32,256]{3,2,0,1:T(8,128)S(1)} collective-permute-done((f32[4,2,32,256]{3,2,0,1:T(8,128)}, f32[4,2,32,256]{3,2,0,1:T(8,128)S(1)}, u32[]{:S(2)}, u32[]{:S(2)}) %collective-permute-start.1) | collective-permute-done | bytes 262176 | tf_op jit(solution)/shard_map/while/body/eval_jaxpr/ppermute | solution.py:12
  486.7 7.5 %collective-permute-done.1 = f32[4,2,32,256]{3,2,0,1:T(8,128)S(1)} collective-permute-done((f32[4,2,32,256]{3,2,0,1:T(8,128)}, f32[4,2,32,256]{3,2,0,1:T(8,128)S(1)}, u32[]{:S(2)}, u32[]{:S(2)}) %collective-permute-start.1) | collective-permute-done | bytes 262176 | tf_op jit(solution)/shard_map/while/body/eval_jaxpr/ppermute | solution.py:12
  494.3 18.5 %while.109 = (s32[]{:T(128)}, f32[4,2,32,256]{3,2,0,1:T(8,128)S(1)}, f32[2,4,2,32,256]{4,1,2,3,0:T(4,128)S(1)}, s32[2]{0:T(128)S(1)}, f32[2,4,2,32,256]{4,3,1,2,...) while((s32[]{:T(128)}, f32[4,2,32,256]{3,2,0,1:T(8,128)S(1)}, ...), condition=%wide.region_15.16_spmd, body=%wide.region_14.15_spmd.sunk | while | flops 604307456 | bytes 14680271 | solution.py:72
  515.3 8.2 %collective-permute-start.3 = (f32[32,256]{1,0:T(8,128)S(1)}, f32[32,256]{1,0:T(8,128)S(1)}, u32[]{:S(2)}, u32[]{:S(2)}) collective-permute-start(f32[32,256]{1,0:T(8,128)S(1)} %get-tuple-element.827), channel_id=1, source_target_pairs={{0,1},{1,2},{2,3},{3,4},{4,5},{5,6},{6,7},{7,8},{8,9},{9,10},{10,1... | collective-permute-start | bytes 98312 | tf_op jit(solution)/shard_map/ppermute | solution.py:12
  525.7 64.7 %psum.7 = f32[2,32,32]{2,1,0:T(8,128)S(1)} all-reduce(f32[2,32,32]{2,1,0:T(8,128)S(1)} %pad_maximum_fusion.4), channel_id=1, replica_groups=mesh['parts'=2,'chain'=16] {'chain'}, use_global_device_ids=true, to_apply=%region_16.17 | all-reduce | flops 2048 | bytes 16384 | tf_op jit(solution)/shard_map/psum | solution.py:118
  (395 shorter events, 386.5 us)
Async XLA Ops:
  63.9 8.1 %collective-permute-start = (f32[4,2,32,256]{3,2,0,1:T(8,128)}, f32[4,2,32,256]{3,2,0,1:T(8,128)S(1)}, u32[]{:S(2)}, u32[]{:S(2)}) collective-permute-start(f32[4,2,32,256]{3,2,0,1:T(8,128)} %maximum_add_fusion.10), channel_id=1, source_target_pairs={{0,1},{1,2},{2,3},{3,4},{4,5},{5,6},{6,7},{7,8},{8,9},{9,10},{10,1... | collective-permute-start | bytes 786440 | tf_op jit(solution)/shard_map/while/body/eval_jaxpr/ppermute | solution.py:12
  156.1 7.9 %collective-permute-start = (f32[4,2,32,256]{3,2,0,1:T(8,128)}, f32[4,2,32,256]{3,2,0,1:T(8,128)S(1)}, u32[]{:S(2)}, u32[]{:S(2)}) collective-permute-start(f32[4,2,32,256]{3,2,0,1:T(8,128)} %maximum_add_fusion.10), channel_id=1, source_target_pairs={{0,1},{1,2},{2,3},{3,4},{4,5},{5,6},{6,7},{7,8},{8,9},{9,10},{10,1... | collective-permute-start | bytes 786440 | tf_op jit(solution)/shard_map/while/body/eval_jaxpr/ppermute | solution.py:12
  167.7 8.8 %collective-permute-start = (f32[4,2,32,256]{3,2,0,1:T(8,128)}, f32[4,2,32,256]{3,2,0,1:T(8,128)S(1)}, u32[]{:S(2)}, u32[]{:S(2)}) collective-permute-start(f32[4,2,32,256]{3,2,0,1:T(8,128)} %maximum_add_fusion.10), channel_id=1, source_target_pairs={{0,1},{1,2},{2,3},{3,4},{4,5},{5,6},{6,7},{7,8},{8,9},{9,10},{10,1... | collective-permute-start | bytes 786440 | tf_op jit(solution)/shard_map/while/body/eval_jaxpr/ppermute | solution.py:12
  180.1 8.8 %collective-permute-start = (f32[4,2,32,256]{3,2,0,1:T(8,128)}, f32[4,2,32,256]{3,2,0,1:T(8,128)S(1)}, u32[]{:S(2)}, u32[]{:S(2)}) collective-permute-start(f32[4,2,32,256]{3,2,0,1:T(8,128)} %maximum_add_fusion.10), channel_id=1, source_target_pairs={{0,1},{1,2},{2,3},{3,4},{4,5},{5,6},{6,7},{7,8},{8,9},{9,10},{10,1... | collective-permute-start | bytes 786440 | tf_op jit(solution)/shard_map/while/body/eval_jaxpr/ppermute | solution.py:12
  192.5 8.8 %collective-permute-start = (f32[4,2,32,256]{3,2,0,1:T(8,128)}, f32[4,2,32,256]{3,2,0,1:T(8,128)S(1)}, u32[]{:S(2)}, u32[]{:S(2)}) collective-permute-start(f32[4,2,32,256]{3,2,0,1:T(8,128)} %maximum_add_fusion.10), channel_id=1, source_target_pairs={{0,1},{1,2},{2,3},{3,4},{4,5},{5,6},{6,7},{7,8},{8,9},{9,10},{10,1... | collective-permute-start | bytes 786440 | tf_op jit(solution)/shard_map/while/body/eval_jaxpr/ppermute | solution.py:12
  204.9 8.8 %collective-permute-start = (f32[4,2,32,256]{3,2,0,1:T(8,128)}, f32[4,2,32,256]{3,2,0,1:T(8,128)S(1)}, u32[]{:S(2)}, u32[]{:S(2)}) collective-permute-start(f32[4,2,32,256]{3,2,0,1:T(8,128)} %maximum_add_fusion.10), channel_id=1, source_target_pairs={{0,1},{1,2},{2,3},{3,4},{4,5},{5,6},{6,7},{7,8},{8,9},{9,10},{10,1... | collective-permute-start | bytes 786440 | tf_op jit(solution)/shard_map/while/body/eval_jaxpr/ppermute | solution.py:12
  217.3 8.8 %collective-permute-start = (f32[4,2,32,256]{3,2,0,1:T(8,128)}, f32[4,2,32,256]{3,2,0,1:T(8,128)S(1)}, u32[]{:S(2)}, u32[]{:S(2)}) collective-permute-start(f32[4,2,32,256]{3,2,0,1:T(8,128)} %maximum_add_fusion.10), channel_id=1, source_target_pairs={{0,1},{1,2},{2,3},{3,4},{4,5},{5,6},{6,7},{7,8},{8,9},{9,10},{10,1... | collective-permute-start | bytes 786440 | tf_op jit(solution)/shard_map/while/body/eval_jaxpr/ppermute | solution.py:12
  297.6 8.7 %collective-permute-start.1 = (f32[4,2,32,256]{3,2,0,1:T(8,128)}, f32[4,2,32,256]{3,2,0,1:T(8,128)S(1)}, u32[]{:S(2)}, u32[]{:S(2)}) collective-permute-start(f32[4,2,32,256]{3,2,0,1:T(8,128)} %maximum_add_fusion.11), channel_id=1, source_target_pairs={{1,0},{2,1},{3,2},{4,3},{5,4},{6,5},{7,6},{8,7},{9,8},{10,9},{11,1... | collective-permute-start | bytes 786440 | tf_op jit(solution)/shard_map/while/body/eval_jaxpr/ppermute | solution.py:12
  310.9 9.4 %collective-permute-start.1 = (f32[4,2,32,256]{3,2,0,1:T(8,128)}, f32[4,2,32,256]{3,2,0,1:T(8,128)S(1)}, u32[]{:S(2)}, u32[]{:S(2)}) collective-permute-start(f32[4,2,32,256]{3,2,0,1:T(8,128)} %maximum_add_fusion.11), channel_id=1, source_target_pairs={{1,0},{2,1},{3,2},{4,3},{5,4},{6,5},{7,6},{8,7},{9,8},{10,9},{11,1... | collective-permute-start | bytes 786440 | tf_op jit(solution)/shard_map/while/body/eval_jaxpr/ppermute | solution.py:12
  324.8 8.7 %collective-permute-start.1 = (f32[4,2,32,256]{3,2,0,1:T(8,128)}, f32[4,2,32,256]{3,2,0,1:T(8,128)S(1)}, u32[]{:S(2)}, u32[]{:S(2)}) collective-permute-start(f32[4,2,32,256]{3,2,0,1:T(8,128)} %maximum_add_fusion.11), channel_id=1, source_target_pairs={{1,0},{2,1},{3,2},{4,3},{5,4},{6,5},{7,6},{8,7},{9,8},{10,9},{11,1... | collective-permute-start | bytes 786440 | tf_op jit(solution)/shard_map/while/body/eval_jaxpr/ppermute | solution.py:12
  338.0 9.4 %collective-permute-start.1 = (f32[4,2,32,256]{3,2,0,1:T(8,128)}, f32[4,2,32,256]{3,2,0,1:T(8,128)S(1)}, u32[]{:S(2)}, u32[]{:S(2)}) collective-permute-start(f32[4,2,32,256]{3,2,0,1:T(8,128)} %maximum_add_fusion.11), channel_id=1, source_target_pairs={{1,0},{2,1},{3,2},{4,3},{5,4},{6,5},{7,6},{8,7},{9,8},{10,9},{11,1... | collective-permute-start | bytes 786440 | tf_op jit(solution)/shard_map/while/body/eval_jaxpr/ppermute | solution.py:12
  352.0 8.8 %collective-permute-start.1 = (f32[4,2,32,256]{3,2,0,1:T(8,128)}, f32[4,2,32,256]{3,2,0,1:T(8,128)S(1)}, u32[]{:S(2)}, u32[]{:S(2)}) collective-permute-start(f32[4,2,32,256]{3,2,0,1:T(8,128)} %maximum_add_fusion.11), channel_id=1, source_target_pairs={{1,0},{2,1},{3,2},{4,3},{5,4},{6,5},{7,6},{8,7},{9,8},{10,9},{11,1... | collective-permute-start | bytes 786440 | tf_op jit(solution)/shard_map/while/body/eval_jaxpr/ppermute | solution.py:12
  365.4 8.8 %collective-permute-start.1 = (f32[4,2,32,256]{3,2,0,1:T(8,128)}, f32[4,2,32,256]{3,2,0,1:T(8,128)S(1)}, u32[]{:S(2)}, u32[]{:S(2)}) collective-permute-start(f32[4,2,32,256]{3,2,0,1:T(8,128)} %maximum_add_fusion.11), channel_id=1, source_target_pairs={{1,0},{2,1},{3,2},{4,3},{5,4},{6,5},{7,6},{8,7},{9,8},{10,9},{11,1... | collective-permute-start | bytes 786440 | tf_op jit(solution)/shard_map/while/body/eval_jaxpr/ppermute | solution.py:12
  378.7 8.8 %collective-permute-start.1 = (f32[4,2,32,256]{3,2,0,1:T(8,128)}, f32[4,2,32,256]{3,2,0,1:T(8,128)S(1)}, u32[]{:S(2)}, u32[]{:S(2)}) collective-permute-start(f32[4,2,32,256]{3,2,0,1:T(8,128)} %maximum_add_fusion.11), channel_id=1, source_target_pairs={{1,0},{2,1},{3,2},{4,3},{5,4},{6,5},{7,6},{8,7},{9,8},{10,9},{11,1... | collective-permute-start | bytes 786440 | tf_op jit(solution)/shard_map/while/body/eval_jaxpr/ppermute | solution.py:12
  392.0 8.8 %collective-permute-start.1 = (f32[4,2,32,256]{3,2,0,1:T(8,128)}, f32[4,2,32,256]{3,2,0,1:T(8,128)S(1)}, u32[]{:S(2)}, u32[]{:S(2)}) collective-permute-start(f32[4,2,32,256]{3,2,0,1:T(8,128)} %maximum_add_fusion.11), channel_id=1, source_target_pairs={{1,0},{2,1},{3,2},{4,3},{5,4},{6,5},{7,6},{8,7},{9,8},{10,9},{11,1... | collective-permute-start | bytes 786440 | tf_op jit(solution)/shard_map/while/body/eval_jaxpr/ppermute | solution.py:12
  405.4 8.8 %collective-permute-start.1 = (f32[4,2,32,256]{3,2,0,1:T(8,128)}, f32[4,2,32,256]{3,2,0,1:T(8,128)S(1)}, u32[]{:S(2)}, u32[]{:S(2)}) collective-permute-start(f32[4,2,32,256]{3,2,0,1:T(8,128)} %maximum_add_fusion.11), channel_id=1, source_target_pairs={{1,0},{2,1},{3,2},{4,3},{5,4},{6,5},{7,6},{8,7},{9,8},{10,9},{11,1... | collective-permute-start | bytes 786440 | tf_op jit(solution)/shard_map/while/body/eval_jaxpr/ppermute | solution.py:12
  418.7 8.8 %collective-permute-start.1 = (f32[4,2,32,256]{3,2,0,1:T(8,128)}, f32[4,2,32,256]{3,2,0,1:T(8,128)S(1)}, u32[]{:S(2)}, u32[]{:S(2)}) collective-permute-start(f32[4,2,32,256]{3,2,0,1:T(8,128)} %maximum_add_fusion.11), channel_id=1, source_target_pairs={{1,0},{2,1},{3,2},{4,3},{5,4},{6,5},{7,6},{8,7},{9,8},{10,9},{11,1... | collective-permute-start | bytes 786440 | tf_op jit(solution)/shard_map/while/body/eval_jaxpr/ppermute | solution.py:12
  432.0 8.8 %collective-permute-start.1 = (f32[4,2,32,256]{3,2,0,1:T(8,128)}, f32[4,2,32,256]{3,2,0,1:T(8,128)S(1)}, u32[]{:S(2)}, u32[]{:S(2)}) collective-permute-start(f32[4,2,32,256]{3,2,0,1:T(8,128)} %maximum_add_fusion.11), channel_id=1, source_target_pairs={{1,0},{2,1},{3,2},{4,3},{5,4},{6,5},{7,6},{8,7},{9,8},{10,9},{11,1... | collective-permute-start | bytes 786440 | tf_op jit(solution)/shard_map/while/body/eval_jaxpr/ppermute | solution.py:12
  445.4 8.8 %collective-permute-start.1 = (f32[4,2,32,256]{3,2,0,1:T(8,128)}, f32[4,2,32,256]{3,2,0,1:T(8,128)S(1)}, u32[]{:S(2)}, u32[]{:S(2)}) collective-permute-start(f32[4,2,32,256]{3,2,0,1:T(8,128)} %maximum_add_fusion.11), channel_id=1, source_target_pairs={{1,0},{2,1},{3,2},{4,3},{5,4},{6,5},{7,6},{8,7},{9,8},{10,9},{11,1... | collective-permute-start | bytes 786440 | tf_op jit(solution)/shard_map/while/body/eval_jaxpr/ppermute | solution.py:12
  458.7 8.8 %collective-permute-start.1 = (f32[4,2,32,256]{3,2,0,1:T(8,128)}, f32[4,2,32,256]{3,2,0,1:T(8,128)S(1)}, u32[]{:S(2)}, u32[]{:S(2)}) collective-permute-start(f32[4,2,32,256]{3,2,0,1:T(8,128)} %maximum_add_fusion.11), channel_id=1, source_target_pairs={{1,0},{2,1},{3,2},{4,3},{5,4},{6,5},{7,6},{8,7},{9,8},{10,9},{11,1... | collective-permute-start | bytes 786440 | tf_op jit(solution)/shard_map/while/body/eval_jaxpr/ppermute | solution.py:12
  472.0 8.8 %collective-permute-start.1 = (f32[4,2,32,256]{3,2,0,1:T(8,128)}, f32[4,2,32,256]{3,2,0,1:T(8,128)S(1)}, u32[]{:S(2)}, u32[]{:S(2)}) collective-permute-start(f32[4,2,32,256]{3,2,0,1:T(8,128)} %maximum_add_fusion.11), channel_id=1, source_target_pairs={{1,0},{2,1},{3,2},{4,3},{5,4},{6,5},{7,6},{8,7},{9,8},{10,9},{11,1... | collective-permute-start | bytes 786440 | tf_op jit(solution)/shard_map/while/body/eval_jaxpr/ppermute | solution.py:12
  485.4 8.8 %collective-permute-start.1 = (f32[4,2,32,256]{3,2,0,1:T(8,128)}, f32[4,2,32,256]{3,2,0,1:T(8,128)S(1)}, u32[]{:S(2)}, u32[]{:S(2)}) collective-permute-start(f32[4,2,32,256]{3,2,0,1:T(8,128)} %maximum_add_fusion.11), channel_id=1, source_target_pairs={{1,0},{2,1},{3,2},{4,3},{5,4},{6,5},{7,6},{8,7},{9,8},{10,9},{11,1... | collective-permute-start | bytes 786440 | tf_op jit(solution)/shard_map/while/body/eval_jaxpr/ppermute | solution.py:12
  513.5 11.3 %collective-permute-start.2 = (f32[32,256]{1,0:T(8,128)S(1)}, f32[32,256]{1,0:T(8,128)S(1)}, u32[]{:S(2)}, u32[]{:S(2)}) collective-permute-start(f32[32,256]{1,0:T(8,128)S(1)} %get-tuple-element.830), channel_id=1, source_target_pairs={{1,0},{2,1},{3,2},{4,3},{5,4},{6,5},{7,6},{8,7},{9,8},{10,9},{11,1... | collective-permute-start | bytes 98312 | tf_op jit(solution)/shard_map/ppermute | solution.py:12
  515.3 9.6 %collective-permute-start.3 = (f32[32,256]{1,0:T(8,128)S(1)}, f32[32,256]{1,0:T(8,128)S(1)}, u32[]{:S(2)}, u32[]{:S(2)}) collective-permute-start(f32[32,256]{1,0:T(8,128)S(1)} %get-tuple-element.827), channel_id=1, source_target_pairs={{0,1},{1,2},{2,3},{3,4},{4,5},{5,6},{6,7},{7,8},{8,9},{9,10},{10,1... | collective-permute-start | bytes 98312 | tf_op jit(solution)/shard_map/ppermute | solution.py:12
  (38 other events, 695.1 us)
where the time goes:
time: 601 us; the launch traced here: 592 us
  matrix products  161 us (27%)
  waiting for transfers between devices  134 us (22%)
  starting transfers between devices  127 us (21%)
  blocking collectives  64.7 us (11%)
  local copies, waits for them, and re-layouts  39.9 us (7%)
  other arithmetic  39.4 us (7%)
  loops' own time  25.1 us (4%)
    ppermute x32, waiting for transfers between devices, passed_along(): return lax.ppermute(shard, axis, pairs)  134 us
    ppermute x32, starting transfers between devices, passed_along(): return lax.ppermute(shard, axis, pairs)  127 us
    psum x1, blocking collectives, shards(): summed = lax.psum(jnp.stack([gram_plain, gram_matrix]), 'chain')  64.7 us
    add x15, other arithmetic, backward_hop(): right_apply(inbound, backward_map) + backward_tip  25.5 us
    dot_general x30, matrix products, right_apply(): jnp.einsum('qnk,qkj->qnj', vecs[:, 1], matrix[:, 0], precision=highest)  21.1 us
    dot_general x30, matrix products, right_apply(): jnp.einsum('qnk,qkj->qnj', vecs[:, 1], matrix[:, 1], precision=highest)  21.1 us
    dot_general x30, matrix products, right_apply(): jnp.einsum('qnk,qkj->qnj', vecs[:, 0], matrix[:, 0], precision=highest)  21.1 us
    dot_general x30, matrix products, right_apply(): jnp.einsum('qnk,qkj->qnj', vecs[:, 0], matrix[:, 1], precision=highest)  21.1 us
  transfers between devices with their start and end apart: 32, of which 30 were waited for; matrix products, arithmetic and copies ran while one was open for 0% of the time, Pallas kernels for 0%

commit v1 on v0

--- a/solution.py
+++ b/solution.py
@@ -115,7 +115,7 @@
     applied_blocks = diag_term + term_up + lower_rows
     gram_plain = jnp.einsum("rnk,rmk->nm", filtered_blocks, filtered_blocks, precision=highest)
     gram_matrix = jnp.einsum("rnk,rmk->nm", filtered_blocks, applied_blocks, precision=highest)
-    summed = lax.psum(jnp.stack([gram_plain, gram_matrix]), "chain")
+    summed = jnp.sum(lax.all_gather(jnp.stack([gram_plain, gram_matrix]), "chain"), axis=0)
     grams = summed / (blocks_dev * block_width * chain_size)
     filtered = filtered_blocks.transpose(1, 0, 2).reshape(vectors, blocks_dev * block_width)
     applied = applied_blocks.transpose(1, 0, 2).reshape(vectors, blocks_dev * block_width)

time: 601 us -> 566 us (0.942)
  blocking collectives: 64.7 us -> 29.5 us
    psum x1 -> x0, blocking collectives: 64.7 us -> none  [shards(): summed = lax.psum(jnp.stack([gram_plain, gram_matrix]), 'chain')]
    all_gather x0 -> x1, blocking collectives: none -> 29.5 us  [shards(): lax.all_gather(jnp.stack([gram_plain, gram_matrix]), 'chain')]
where the time goes in v1:
time: 566 us; the launch traced here: 557 us
  matrix products  161 us (28%)
  waiting for transfers between devices  134 us (24%)
  starting transfers between devices  127 us (22%)
  local copies, waits for them, and re-layouts  39.9 us (7%)
  other arithmetic  39.4 us (7%)
  blocking collectives  29.5 us (5%)
  loops' own time  25.1 us (4%)
    ppermute x32, waiting for transfers between devices, passed_along(): return lax.ppermute(shard, axis, pairs)  134 us
    ppermute x32, starting transfers between devices, passed_along(): return lax.ppermute(shard, axis, pairs)  127 us
    all_gather x1, blocking collectives, shards(): lax.all_gather(jnp.stack([gram_plain, gram_matrix]), 'chain')  29.5 us
    add x15, other arithmetic, backward_hop(): right_apply(inbound, backward_map) + backward_tip  25.5 us
    dot_general x30, matrix products, right_apply(): jnp.einsum('qnk,qkj->qnj', vecs[:, 1], matrix[:, 0], precision=highest)  21.1 us
    dot_general x30, matrix products, right_apply(): jnp.einsum('qnk,qkj->qnj', vecs[:, 1], matrix[:, 1], precision=highest)  21.1 us
    dot_general x30, matrix products, right_apply(): jnp.einsum('qnk,qkj->qnj', vecs[:, 0], matrix[:, 0], precision=highest)  21.1 us
    dot_general x30, matrix products, right_apply(): jnp.einsum('qnk,qkj->qnj', vecs[:, 0], matrix[:, 1], precision=highest)  21.1 us
  transfers between devices with their start and end apart: 32, of which 30 were waited for; matrix products, arithmetic and copies ran while one was open for 0% of the time, Pallas kernels for 0%

profile of v1, /device:TPU:0, one launch (start us, length us, event | category | flops | bytes accessed | tf_op | source)
XLA Modules:
  0.0 556.7 jit_solution(12103806369253063120)
XLA Ops:
  6.5 25.1 %while.104 = (s32[]{:T(128)}, f32[4,2,256,256]{3,2,1,0:T(8,128)S(1)}, s32[2]{0:T(128)S(1)}, f32[4,2,2,256,256]{4,3,0,2,1:T(8,128)}, f32[2,256,256]{2,1,0:T(8,128)S(1)}, /*index=5*/s32[]{:T(128)}, s32[]{:T(128)}, s32[]{:T(128)}) while((s32[]{:T(128)}, f32[4,2,256,256]{3,2,1,0:T(8,128)S(1)}, s32[2]{0:T(128)S(1)}, ...), condition=%wide.region_3.4_spmd, body=%wide.region_2.3_spmd.sunk | while | flops 4832886784 | bytes 23330956 | solution.py:56
  33.3 18.8 %while.105 = (s32[]{:T(128)}, f32[4,2,32,256]{3,2,1,0:T(8,128)S(1)}, s32[2]{0:T(128)S(1)}, f32[2,32,256]{2,1,0:T(8,128)S(1)}, f32[4,2,2,256,256]{4,3,0,2,1:T(8,1...) while((s32[]{:T(128)}, f32[4,2,32,256]{3,2,1,0:T(8,128)S(1)}, s32[2]{0:T(128)S(1)}, ...), condition=%wide.region_5.6_spmd, body=%wide.region_4.5_spmd.sunk | while | flops 604176384 | bytes 10616983 | solution.py:56
  52.9 173.2 %while.106 = (s32[]{:T(128)}, f32[4,2,32,256]{3,2,0,1:T(8,128)S(1)}, f32[4,2,256,256]{3,2,0,1:T(8,128)S(1)}, f32[4,2,32,256]{3,2,0,1:T(8,128)}, s32[]{:T(128)}) while((s32[]{:T(128)}, f32[4,2,32,256]{3,2,0,1:T(8,128)S(1)}, f32[4,2,256,256]{3,2,0,1:T(8,128)S(1)}, f32[4,2,32,256]{3,2,0,1:T(8,128)}, s32[]{:T(128)}) %tuple.243), condition=%wide.region_7.8_spmd, body=%wide.region_6.7_spmd.sunk | while | flops 402849792 | bytes 8388737 | solution.py:96
  167.7 7.4 %collective-permute-start = (f32[4,2,32,256]{3,2,0,1:T(8,128)}, f32[4,2,32,256]{3,2,0,1:T(8,128)S(1)}, u32[]{:S(2)}, u32[]{:S(2)}) collective-permute-start(f32[4,2,32,256]{3,2,0,1:T(8,128)} %maximum_add_fusion.10), channel_id=1, source_target_pairs={{0,1},{1,2},{2,3},{3,4},{4,5},{5,6},{6,7},{7,8},{8,9},{9,10},{10,1... | collective-permute-start | bytes 786440 | tf_op jit(solution)/shard_map/while/body/eval_jaxpr/ppermute | solution.py:12
  226.1 18.2 %while.107 = (s32[]{:T(128)}, f32[4,2,32,256]{3,2,1,0:T(8,128)S(1)}, f32[2,4,2,32,256]{4,3,1,2,0:T(8,128)}, s32[2]{0:T(128)S(1)}, f32[2,32,256]{2,1,0:T(8,128)S(...) while((s32[]{:T(128)}, f32[4,2,32,256]{3,2,1,0:T(8,128)S(1)}, ...), condition=%wide.region_9.10_spmd, body=%wide.region_8.9_spmd.sunk | while | flops 604241920 | bytes 15335643 | solution.py:56
  244.3 19.8 %while.110 = (s32[]{:T(128)}, f32[4,2,32,256]{3,2,0,1:T(8,128)}, s32[2]{0:T(128)S(1)}, f32[2,4,2,32,256]{4,3,1,2,0:T(8,128)}, f32[2,256,256]{2,1,0:T(8,128)S(1)}...) while((s32[]{:T(128)}, f32[4,2,32,256]{3,2,0,1:T(8,128)}, ...), condition=%wide.region_11.12_spmd.clone, body=%wide.region_10.11_spmd.clone.sunk | while | flops 604241920 | bytes 13369545 | solution.py:72
  265.3 27.5 %while.103 = (s32[]{:T(128)}, f32[4,2,256,256]{3,2,0,1:T(8,128)S(1)}, s32[2]{0:T(128)S(1)}, f32[2,256,256]{2,1,0:T(8,128)S(1)}, f32[4,2,2,256,256]{4,3,0,2,1:T(8,128)}, /*index=5*/s32[]{:T(128)}, s32[]{:T(128)}, s32[]{:T(128)}) while((s32[]{:T(128)}, f32[4,2,256,256]{3,2,0,1:T(8,128)S(1)}, s32[2]{0:T(128)S(1)}, f32[2,256,256]{2,1,0:T(8,128)S(1)}, ...), condition=%wide.region_1.2_spmd, body=%wide.region_0.1_spmd.sunk | while | flops 4832886784 | bytes 27525272 | solution.py:72
  292.9 201.3 %while.108 = (s32[]{:T(128)}, f32[4,2,32,256]{3,2,0,1:T(8,128)S(1)}, f32[4,2,256,256]{3,2,0,1:T(8,128)S(1)}, f32[4,2,32,256]{3,2,0,1:T(8,128)}, s32[]{:T(128)}) while((s32[]{:T(128)}, f32[4,2,32,256]{3,2,0,1:T(8,128)S(1)}, f32[4,2,256,256]{3,2,0,1:T(8,128)S(1)}, f32[4,2,32,256]{3,2,0,1:T(8,128)}, s32[]{:T(128)}) %tuple.232), condition=%wide.region_13.14_spmd, body=%wide.region_12.13_spmd.sunk | while | flops 402849792 | bytes 7340133 | solution.py:104
  312.2 8.1 %collective-permute-done.1 = f32[4,2,32,256]{3,2,0,1:T(8,128)S(1)} collective-permute-done((f32[4,2,32,256]{3,2,0,1:T(8,128)}, f32[4,2,32,256]{3,2,0,1:T(8,128)S(1)}, u32[]{:S(2)}, u32[]{:S(2)}) %collective-permute-start.1) | collective-permute-done | bytes 262176 | tf_op jit(solution)/shard_map/while/body/eval_jaxpr/ppermute | solution.py:12
  339.3 8.1 %collective-permute-done.1 = f32[4,2,32,256]{3,2,0,1:T(8,128)S(1)} collective-permute-done((f32[4,2,32,256]{3,2,0,1:T(8,128)}, f32[4,2,32,256]{3,2,0,1:T(8,128)S(1)}, u32[]{:S(2)}, u32[]{:S(2)}) %collective-permute-start.1) | collective-permute-done | bytes 262176 | tf_op jit(solution)/shard_map/while/body/eval_jaxpr/ppermute | solution.py:12
  353.3 7.5 %collective-permute-done.1 = f32[4,2,32,256]{3,2,0,1:T(8,128)S(1)} collective-permute-done((f32[4,2,32,256]{3,2,0,1:T(8,128)}, f32[4,2,32,256]{3,2,0,1:T(8,128)S(1)}, u32[]{:S(2)}, u32[]{:S(2)}) %collective-permute-start.1) | collective-permute-done | bytes 262176 | tf_op jit(solution)/shard_map/while/body/eval_jaxpr/ppermute | solution.py:12
  366.6 7.5 %collective-permute-done.1 = f32[4,2,32,256]{3,2,0,1:T(8,128)S(1)} collective-permute-done((f32[4,2,32,256]{3,2,0,1:T(8,128)}, f32[4,2,32,256]{3,2,0,1:T(8,128)S(1)}, u32[]{:S(2)}, u32[]{:S(2)}) %collective-permute-start.1) | collective-permute-done | bytes 262176 | tf_op jit(solution)/shard_map/while/body/eval_jaxpr/ppermute | solution.py:12
  380.0 7.5 %collective-permute-done.1 = f32[4,2,32,256]{3,2,0,1:T(8,128)S(1)} collective-permute-done((f32[4,2,32,256]{3,2,0,1:T(8,128)}, f32[4,2,32,256]{3,2,0,1:T(8,128)S(1)}, u32[]{:S(2)}, u32[]{:S(2)}) %collective-permute-start.1) | collective-permute-done | bytes 262176 | tf_op jit(solution)/shard_map/while/body/eval_jaxpr/ppermute | solution.py:12
  393.3 7.5 %collective-permute-done.1 = f32[4,2,32,256]{3,2,0,1:T(8,128)S(1)} collective-permute-done((f32[4,2,32,256]{3,2,0,1:T(8,128)}, f32[4,2,32,256]{3,2,0,1:T(8,128)S(1)}, u32[]{:S(2)}, u32[]{:S(2)}) %collective-permute-start.1) | collective-permute-done | bytes 262176 | tf_op jit(solution)/shard_map/while/body/eval_jaxpr/ppermute | solution.py:12
  406.7 7.5 %collective-permute-done.1 = f32[4,2,32,256]{3,2,0,1:T(8,128)S(1)} collective-permute-done((f32[4,2,32,256]{3,2,0,1:T(8,128)}, f32[4,2,32,256]{3,2,0,1:T(8,128)S(1)}, u32[]{:S(2)}, u32[]{:S(2)}) %collective-permute-start.1) | collective-permute-done | bytes 262176 | tf_op jit(solution)/shard_map/while/body/eval_jaxpr/ppermute | solution.py:12
  420.0 7.5 %collective-permute-done.1 = f32[4,2,32,256]{3,2,0,1:T(8,128)S(1)} collective-permute-done((f32[4,2,32,256]{3,2,0,1:T(8,128)}, f32[4,2,32,256]{3,2,0,1:T(8,128)S(1)}, u32[]{:S(2)}, u32[]{:S(2)}) %collective-permute-start.1) | collective-permute-done | bytes 262176 | tf_op jit(solution)/shard_map/while/body/eval_jaxpr/ppermute | solution.py:12
  433.3 7.5 %collective-permute-done.1 = f32[4,2,32,256]{3,2,0,1:T(8,128)S(1)} collective-permute-done((f32[4,2,32,256]{3,2,0,1:T(8,128)}, f32[4,2,32,256]{3,2,0,1:T(8,128)S(1)}, u32[]{:S(2)}, u32[]{:S(2)}) %collective-permute-start.1) | collective-permute-done | bytes 262176 | tf_op jit(solution)/shard_map/while/body/eval_jaxpr/ppermute | solution.py:12
  446.7 7.5 %collective-permute-done.1 = f32[4,2,32,256]{3,2,0,1:T(8,128)S(1)} collective-permute-done((f32[4,2,32,256]{3,2,0,1:T(8,128)}, f32[4,2,32,256]{3,2,0,1:T(8,128)S(1)}, u32[]{:S(2)}, u32[]{:S(2)}) %collective-permute-start.1) | collective-permute-done | bytes 262176 | tf_op jit(solution)/shard_map/while/body/eval_jaxpr/ppermute | solution.py:12
  460.0 7.5 %collective-permute-done.1 = f32[4,2,32,256]{3,2,0,1:T(8,128)S(1)} collective-permute-done((f32[4,2,32,256]{3,2,0,1:T(8,128)}, f32[4,2,32,256]{3,2,0,1:T(8,128)S(1)}, u32[]{:S(2)}, u32[]{:S(2)}) %collective-permute-start.1) | collective-permute-done | bytes 262176 | tf_op jit(solution)/shard_map/while/body/eval_jaxpr/ppermute | solution.py:12
  473.3 7.5 %collective-permute-done.1 = f32[4,2,32,256]{3,2,0,1:T(8,128)S(1)} collective-permute-done((f32[4,2,32,256]{3,2,0,1:T(8,128)}, f32[4,2,32,256]{3,2,0,1:T(8,128)S(1)}, u32[]{:S(2)}, u32[]{:S(2)}) %collective-permute-start.1) | collective-permute-done | bytes 262176 | tf_op jit(solution)/shard_map/while/body/eval_jaxpr/ppermute | solution.py:12
  486.7 7.5 %collective-permute-done.1 = f32[4,2,32,256]{3,2,0,1:T(8,128)S(1)} collective-permute-done((f32[4,2,32,256]{3,2,0,1:T(8,128)}, f32[4,2,32,256]{3,2,0,1:T(8,128)S(1)}, u32[]{:S(2)}, u32[]{:S(2)}) %collective-permute-start.1) | collective-permute-done | bytes 262176 | tf_op jit(solution)/shard_map/while/body/eval_jaxpr/ppermute | solution.py:12
  494.3 18.5 %while.109 = (s32[]{:T(128)}, f32[4,2,32,256]{3,2,0,1:T(8,128)S(1)}, f32[2,4,2,32,256]{4,1,2,3,0:T(4,128)S(1)}, s32[2]{0:T(128)S(1)}, f32[2,4,2,32,256]{4,3,1,2,...) while((s32[]{:T(128)}, f32[4,2,32,256]{3,2,0,1:T(8,128)S(1)}, ...), condition=%wide.region_15.16_spmd, body=%wide.region_14.15_spmd.sunk | while | flops 604307456 | bytes 14680271 | solution.py:72
  515.3 8.2 %collective-permute-start.3 = (f32[32,256]{1,0:T(8,128)S(1)}, f32[32,256]{1,0:T(8,128)S(1)}, u32[]{:S(2)}, u32[]{:S(2)}) collective-permute-start(f32[32,256]{1,0:T(8,128)S(1)} %get-tuple-element.867), channel_id=1, source_target_pairs={{0,1},{1,2},{2,3},{3,4},{4,5},{5,6},{6,7},{7,8},{8,9},{9,10},{10,1... | collective-permute-start | bytes 98312 | tf_op jit(solution)/shard_map/ppermute | solution.py:12
  525.7 29.5 %all-gather = f32[32,32,32]{2,1,0:T(8,128)S(1)} all-gather(f32[2,32,32]{2,1,0:T(8,128)S(1)} %pad_maximum_fusion.4), channel_id=2, replica_groups=mesh['parts'=2,'chain'=16] {'chain'}, dimensions={0}, use_global_device_ids=true | all-gather | bytes 139264 | tf_op jit(solution)/shard_map/all_gather | solution.py:118
  (396 shorter events, 386.5 us)
Async XLA Ops:
  63.9 8.1 %collective-permute-start = (f32[4,2,32,256]{3,2,0,1:T(8,128)}, f32[4,2,32,256]{3,2,0,1:T(8,128)S(1)}, u32[]{:S(2)}, u32[]{:S(2)}) collective-permute-start(f32[4,2,32,256]{3,2,0,1:T(8,128)} %maximum_add_fusion.10), channel_id=1, source_target_pairs={{0,1},{1,2},{2,3},{3,4},{4,5},{5,6},{6,7},{7,8},{8,9},{9,10},{10,1... | collective-permute-start | bytes 786440 | tf_op jit(solution)/shard_map/while/body/eval_jaxpr/ppermute | solution.py:12
  156.1 7.9 %collective-permute-start = (f32[4,2,32,256]{3,2,0,1:T(8,128)}, f32[4,2,32,256]{3,2,0,1:T(8,128)S(1)}, u32[]{:S(2)}, u32[]{:S(2)}) collective-permute-start(f32[4,2,32,256]{3,2,0,1:T(8,128)} %maximum_add_fusion.10), channel_id=1, source_target_pairs={{0,1},{1,2},{2,3},{3,4},{4,5},{5,6},{6,7},{7,8},{8,9},{9,10},{10,1... | collective-permute-start | bytes 786440 | tf_op jit(solution)/shard_map/while/body/eval_jaxpr/ppermute | solution.py:12
  167.7 8.8 %collective-permute-start = (f32[4,2,32,256]{3,2,0,1:T(8,128)}, f32[4,2,32,256]{3,2,0,1:T(8,128)S(1)}, u32[]{:S(2)}, u32[]{:S(2)}) collective-permute-start(f32[4,2,32,256]{3,2,0,1:T(8,128)} %maximum_add_fusion.10), channel_id=1, source_target_pairs={{0,1},{1,2},{2,3},{3,4},{4,5},{5,6},{6,7},{7,8},{8,9},{9,10},{10,1... | collective-permute-start | bytes 786440 | tf_op jit(solution)/shard_map/while/body/eval_jaxpr/ppermute | solution.py:12
  180.1 8.8 %collective-permute-start = (f32[4,2,32,256]{3,2,0,1:T(8,128)}, f32[4,2,32,256]{3,2,0,1:T(8,128)S(1)}, u32[]{:S(2)}, u32[]{:S(2)}) collective-permute-start(f32[4,2,32,256]{3,2,0,1:T(8,128)} %maximum_add_fusion.10), channel_id=1, source_target_pairs={{0,1},{1,2},{2,3},{3,4},{4,5},{5,6},{6,7},{7,8},{8,9},{9,10},{10,1... | collective-permute-start | bytes 786440 | tf_op jit(solution)/shard_map/while/body/eval_jaxpr/ppermute | solution.py:12
  192.5 8.8 %collective-permute-start = (f32[4,2,32,256]{3,2,0,1:T(8,128)}, f32[4,2,32,256]{3,2,0,1:T(8,128)S(1)}, u32[]{:S(2)}, u32[]{:S(2)}) collective-permute-start(f32[4,2,32,256]{3,2,0,1:T(8,128)} %maximum_add_fusion.10), channel_id=1, source_target_pairs={{0,1},{1,2},{2,3},{3,4},{4,5},{5,6},{6,7},{7,8},{8,9},{9,10},{10,1... | collective-permute-start | bytes 786440 | tf_op jit(solution)/shard_map/while/body/eval_jaxpr/ppermute | solution.py:12
  204.9 8.8 %collective-permute-start = (f32[4,2,32,256]{3,2,0,1:T(8,128)}, f32[4,2,32,256]{3,2,0,1:T(8,128)S(1)}, u32[]{:S(2)}, u32[]{:S(2)}) collective-permute-start(f32[4,2,32,256]{3,2,0,1:T(8,128)} %maximum_add_fusion.10), channel_id=1, source_target_pairs={{0,1},{1,2},{2,3},{3,4},{4,5},{5,6},{6,7},{7,8},{8,9},{9,10},{10,1... | collective-permute-start | bytes 786440 | tf_op jit(solution)/shard_map/while/body/eval_jaxpr/ppermute | solution.py:12
  217.3 8.8 %collective-permute-start = (f32[4,2,32,256]{3,2,0,1:T(8,128)}, f32[4,2,32,256]{3,2,0,1:T(8,128)S(1)}, u32[]{:S(2)}, u32[]{:S(2)}) collective-permute-start(f32[4,2,32,256]{3,2,0,1:T(8,128)} %maximum_add_fusion.10), channel_id=1, source_target_pairs={{0,1},{1,2},{2,3},{3,4},{4,5},{5,6},{6,7},{7,8},{8,9},{9,10},{10,1... | collective-permute-start | bytes 786440 | tf_op jit(solution)/shard_map/while/body/eval_jaxpr/ppermute | solution.py:12
  297.6 8.7 %collective-permute-start.1 = (f32[4,2,32,256]{3,2,0,1:T(8,128)}, f32[4,2,32,256]{3,2,0,1:T(8,128)S(1)}, u32[]{:S(2)}, u32[]{:S(2)}) collective-permute-start(f32[4,2,32,256]{3,2,0,1:T(8,128)} %maximum_add_fusion.11), channel_id=1, source_target_pairs={{1,0},{2,1},{3,2},{4,3},{5,4},{6,5},{7,6},{8,7},{9,8},{10,9},{11,1... | collective-permute-start | bytes 786440 | tf_op jit(solution)/shard_map/while/body/eval_jaxpr/ppermute | solution.py:12
  310.9 9.4 %collective-permute-start.1 = (f32[4,2,32,256]{3,2,0,1:T(8,128)}, f32[4,2,32,256]{3,2,0,1:T(8,128)S(1)}, u32[]{:S(2)}, u32[]{:S(2)}) collective-permute-start(f32[4,2,32,256]{3,2,0,1:T(8,128)} %maximum_add_fusion.11), channel_id=1, source_target_pairs={{1,0},{2,1},{3,2},{4,3},{5,4},{6,5},{7,6},{8,7},{9,8},{10,9},{11,1... | collective-permute-start | bytes 786440 | tf_op jit(solution)/shard_map/while/body/eval_jaxpr/ppermute | solution.py:12
  324.8 8.7 %collective-permute-start.1 = (f32[4,2,32,256]{3,2,0,1:T(8,128)}, f32[4,2,32,256]{3,2,0,1:T(8,128)S(1)}, u32[]{:S(2)}, u32[]{:S(2)}) collective-permute-start(f32[4,2,32,256]{3,2,0,1:T(8,128)} %maximum_add_fusion.11), channel_id=1, source_target_pairs={{1,0},{2,1},{3,2},{4,3},{5,4},{6,5},{7,6},{8,7},{9,8},{10,9},{11,1... | collective-permute-start | bytes 786440 | tf_op jit(solution)/shard_map/while/body/eval_jaxpr/ppermute | solution.py:12
  338.0 9.4 %collective-permute-start.1 = (f32[4,2,32,256]{3,2,0,1:T(8,128)}, f32[4,2,32,256]{3,2,0,1:T(8,128)S(1)}, u32[]{:S(2)}, u32[]{:S(2)}) collective-permute-start(f32[4,2,32,256]{3,2,0,1:T(8,128)} %maximum_add_fusion.11), channel_id=1, source_target_pairs={{1,0},{2,1},{3,2},{4,3},{5,4},{6,5},{7,6},{8,7},{9,8},{10,9},{11,1... | collective-permute-start | bytes 786440 | tf_op jit(solution)/shard_map/while/body/eval_jaxpr/ppermute | solution.py:12
  352.0 8.8 %collective-permute-start.1 = (f32[4,2,32,256]{3,2,0,1:T(8,128)}, f32[4,2,32,256]{3,2,0,1:T(8,128)S(1)}, u32[]{:S(2)}, u32[]{:S(2)}) collective-permute-start(f32[4,2,32,256]{3,2,0,1:T(8,128)} %maximum_add_fusion.11), channel_id=1, source_target_pairs={{1,0},{2,1},{3,2},{4,3},{5,4},{6,5},{7,6},{8,7},{9,8},{10,9},{11,1... | collective-permute-start | bytes 786440 | tf_op jit(solution)/shard_map/while/body/eval_jaxpr/ppermute | solution.py:12
  365.4 8.8 %collective-permute-start.1 = (f32[4,2,32,256]{3,2,0,1:T(8,128)}, f32[4,2,32,256]{3,2,0,1:T(8,128)S(1)}, u32[]{:S(2)}, u32[]{:S(2)}) collective-permute-start(f32[4,2,32,256]{3,2,0,1:T(8,128)} %maximum_add_fusion.11), channel_id=1, source_target_pairs={{1,0},{2,1},{3,2},{4,3},{5,4},{6,5},{7,6},{8,7},{9,8},{10,9},{11,1... | collective-permute-start | bytes 786440 | tf_op jit(solution)/shard_map/while/body/eval_jaxpr/ppermute | solution.py:12
  378.7 8.8 %collective-permute-start.1 = (f32[4,2,32,256]{3,2,0,1:T(8,128)}, f32[4,2,32,256]{3,2,0,1:T(8,128)S(1)}, u32[]{:S(2)}, u32[]{:S(2)}) collective-permute-start(f32[4,2,32,256]{3,2,0,1:T(8,128)} %maximum_add_fusion.11), channel_id=1, source_target_pairs={{1,0},{2,1},{3,2},{4,3},{5,4},{6,5},{7,6},{8,7},{9,8},{10,9},{11,1... | collective-permute-start | bytes 786440 | tf_op jit(solution)/shard_map/while/body/eval_jaxpr/ppermute | solution.py:12
  392.0 8.8 %collective-permute-start.1 = (f32[4,2,32,256]{3,2,0,1:T(8,128)}, f32[4,2,32,256]{3,2,0,1:T(8,128)S(1)}, u32[]{:S(2)}, u32[]{:S(2)}) collective-permute-start(f32[4,2,32,256]{3,2,0,1:T(8,128)} %maximum_add_fusion.11), channel_id=1, source_target_pairs={{1,0},{2,1},{3,2},{4,3},{5,4},{6,5},{7,6},{8,7},{9,8},{10,9},{11,1... | collective-permute-start | bytes 786440 | tf_op jit(solution)/shard_map/while/body/eval_jaxpr/ppermute | solution.py:12
  405.4 8.8 %collective-permute-start.1 = (f32[4,2,32,256]{3,2,0,1:T(8,128)}, f32[4,2,32,256]{3,2,0,1:T(8,128)S(1)}, u32[]{:S(2)}, u32[]{:S(2)}) collective-permute-start(f32[4,2,32,256]{3,2,0,1:T(8,128)} %maximum_add_fusion.11), channel_id=1, source_target_pairs={{1,0},{2,1},{3,2},{4,3},{5,4},{6,5},{7,6},{8,7},{9,8},{10,9},{11,1... | collective-permute-start | bytes 786440 | tf_op jit(solution)/shard_map/while/body/eval_jaxpr/ppermute | solution.py:12
  418.7 8.8 %collective-permute-start.1 = (f32[4,2,32,256]{3,2,0,1:T(8,128)}, f32[4,2,32,256]{3,2,0,1:T(8,128)S(1)}, u32[]{:S(2)}, u32[]{:S(2)}) collective-permute-start(f32[4,2,32,256]{3,2,0,1:T(8,128)} %maximum_add_fusion.11), channel_id=1, source_target_pairs={{1,0},{2,1},{3,2},{4,3},{5,4},{6,5},{7,6},{8,7},{9,8},{10,9},{11,1... | collective-permute-start | bytes 786440 | tf_op jit(solution)/shard_map/while/body/eval_jaxpr/ppermute | solution.py:12
  432.0 8.8 %collective-permute-start.1 = (f32[4,2,32,256]{3,2,0,1:T(8,128)}, f32[4,2,32,256]{3,2,0,1:T(8,128)S(1)}, u32[]{:S(2)}, u32[]{:S(2)}) collective-permute-start(f32[4,2,32,256]{3,2,0,1:T(8,128)} %maximum_add_fusion.11), channel_id=1, source_target_pairs={{1,0},{2,1},{3,2},{4,3},{5,4},{6,5},{7,6},{8,7},{9,8},{10,9},{11,1... | collective-permute-start | bytes 786440 | tf_op jit(solution)/shard_map/while/body/eval_jaxpr/ppermute | solution.py:12
  445.4 8.8 %collective-permute-start.1 = (f32[4,2,32,256]{3,2,0,1:T(8,128)}, f32[4,2,32,256]{3,2,0,1:T(8,128)S(1)}, u32[]{:S(2)}, u32[]{:S(2)}) collective-permute-start(f32[4,2,32,256]{3,2,0,1:T(8,128)} %maximum_add_fusion.11), channel_id=1, source_target_pairs={{1,0},{2,1},{3,2},{4,3},{5,4},{6,5},{7,6},{8,7},{9,8},{10,9},{11,1... | collective-permute-start | bytes 786440 | tf_op jit(solution)/shard_map/while/body/eval_jaxpr/ppermute | solution.py:12
  458.7 8.8 %collective-permute-start.1 = (f32[4,2,32,256]{3,2,0,1:T(8,128)}, f32[4,2,32,256]{3,2,0,1:T(8,128)S(1)}, u32[]{:S(2)}, u32[]{:S(2)}) collective-permute-start(f32[4,2,32,256]{3,2,0,1:T(8,128)} %maximum_add_fusion.11), channel_id=1, source_target_pairs={{1,0},{2,1},{3,2},{4,3},{5,4},{6,5},{7,6},{8,7},{9,8},{10,9},{11,1... | collective-permute-start | bytes 786440 | tf_op jit(solution)/shard_map/while/body/eval_jaxpr/ppermute | solution.py:12
  472.0 8.8 %collective-permute-start.1 = (f32[4,2,32,256]{3,2,0,1:T(8,128)}, f32[4,2,32,256]{3,2,0,1:T(8,128)S(1)}, u32[]{:S(2)}, u32[]{:S(2)}) collective-permute-start(f32[4,2,32,256]{3,2,0,1:T(8,128)} %maximum_add_fusion.11), channel_id=1, source_target_pairs={{1,0},{2,1},{3,2},{4,3},{5,4},{6,5},{7,6},{8,7},{9,8},{10,9},{11,1... | collective-permute-start | bytes 786440 | tf_op jit(solution)/shard_map/while/body/eval_jaxpr/ppermute | solution.py:12
  485.4 8.8 %collective-permute-start.1 = (f32[4,2,32,256]{3,2,0,1:T(8,128)}, f32[4,2,32,256]{3,2,0,1:T(8,128)S(1)}, u32[]{:S(2)}, u32[]{:S(2)}) collective-permute-start(f32[4,2,32,256]{3,2,0,1:T(8,128)} %maximum_add_fusion.11), channel_id=1, source_target_pairs={{1,0},{2,1},{3,2},{4,3},{5,4},{6,5},{7,6},{8,7},{9,8},{10,9},{11,1... | collective-permute-start | bytes 786440 | tf_op jit(solution)/shard_map/while/body/eval_jaxpr/ppermute | solution.py:12
  513.5 11.3 %collective-permute-start.2 = (f32[32,256]{1,0:T(8,128)S(1)}, f32[32,256]{1,0:T(8,128)S(1)}, u32[]{:S(2)}, u32[]{:S(2)}) collective-permute-start(f32[32,256]{1,0:T(8,128)S(1)} %get-tuple-element.870), channel_id=1, source_target_pairs={{1,0},{2,1},{3,2},{4,3},{5,4},{6,5},{7,6},{8,7},{9,8},{10,9},{11,1... | collective-permute-start | bytes 98312 | tf_op jit(solution)/shard_map/ppermute | solution.py:12
  515.3 9.6 %collective-permute-start.3 = (f32[32,256]{1,0:T(8,128)S(1)}, f32[32,256]{1,0:T(8,128)S(1)}, u32[]{:S(2)}, u32[]{:S(2)}) collective-permute-start(f32[32,256]{1,0:T(8,128)S(1)} %get-tuple-element.867), channel_id=1, source_target_pairs={{0,1},{1,2},{2,3},{3,4},{4,5},{5,6},{6,7},{7,8},{8,9},{9,10},{10,1... | collective-permute-start | bytes 98312 | tf_op jit(solution)/shard_map/ppermute | solution.py:12
  (38 other events, 695.1 us)
